TPU v7x, 512 devices: a whole 4x8x8 slice. The times are simulated.
512 devices in a mesh: slab: 64 (over z, x, core), obs: 8 (over y).
Axes of the slice: x: 4, y: 8, z: 8, core: 2. Of those that a mesh axis runs over, the one named last changes fastest.
Arguments:
- background_members: float32 [64, 1048576], P('slab', 'obs'), may hold values from -6 to 6
- measurement_jitter: bfloat16 [64, 8, 65536], P(None, 'obs', 'slab'), may hold values from -5 to 5
- measurement_readings: float32 [8, 65536], P('obs', 'slab'), may hold values from -8 to 8
- measurement_noise_spread: float32 [8, 65536], P('obs', 'slab'), may hold values from 0.2 to 2
- measurement_grid_location: int32 [8, 65536], P('obs', 'slab'), may hold values from 0 to 2047
- active_tallies: int32 [8, 64], P('obs', 'slab'), may hold values from 128 to 1024, as said below
- coupling_listing: int32 [8, 2048, 8], P('obs', 'slab'), may hold values from 0 to 63, as said below
- taper_factors: float32 [8, 2048, 8], P('obs', 'slab'), may hold values from 0.1 to 1
Outputs:
- analysis: float32 [64, 1048576], P('slab', 'obs')
Inputs may be any that keep to these rules, and one draw needn't show every extreme that they name: `active_tallies`: some region of some group holds 1024 live observations; slots beyond a region's count are padding. `coupling_listing`: the 8 observation blocks listed for a state block are distinct.
All inputs are finite; a program needn't handle non-finite values.
Results may differ from a plain program's by a relative error of at most 0.0063.
Values may be sent and summed in bfloat16 or wider, within the bound.
No kernel may reach another device: no remote copies, remote signals or barrier semaphores. Data moves between devices by JAX's collectives and lax.ppermute only.
A program may use at most 64 MiB of HBM per device.

v0:
```python
import jax
import jax.numpy as jnp
from jax import lax
from jax.sharding import PartitionSpec as P

OB = 128
highest = lax.Precision.HIGHEST


def block_products(
    tile_work,
    measurement_jitter,
    measurement_readings,
    measurement_noise_spread,
    measurement_grid_location,
    active_tallies,
):
    members = tile_work.shape[0]
    positions = measurement_grid_location[0]
    obs_count = positions.shape[0]
    prior_value = jnp.take(tile_work, positions, axis=1)
    prior_shift = prior_value - jnp.mean(prior_value, axis=0, keepdims=True)
    spread = jnp.sum(prior_shift * prior_shift, axis=0, keepdims=True) / (members - 1)
    usable = jnp.arange(obs_count, dtype=jnp.int32)[None, :] < active_tallies[0, 0]
    innovation = (
        measurement_readings + measurement_jitter[:, 0, :].astype(jnp.float32) - prior_value
    ) / (spread + measurement_noise_spread)
    gain_input = jnp.where(usable, innovation, jnp.float32(0.0)).astype(jnp.bfloat16)
    prior_low = prior_shift.astype(jnp.bfloat16)
    return jnp.einsum(
        "mco,nco->cmn",
        gain_input.reshape(members, -1, OB),
        prior_low.reshape(members, -1, OB),
        preferred_element_type=jnp.float32,
    )


def local(
    background_members,
    measurement_jitter,
    measurement_readings,
    measurement_noise_spread,
    measurement_grid_location,
    active_tallies,
    coupling_listing,
    taper_factors,
):
    work_low = background_members.astype(jnp.bfloat16)
    tile_low = lax.all_to_all(work_low, "slab", split_axis=1, concat_axis=0, tiled=True)
    tile_work = tile_low.astype(jnp.float32)
    members = tile_work.shape[0]
    blocks = coupling_listing.shape[1]
    deviation = tile_work - jnp.mean(tile_work, axis=0, keepdims=True)
    products = block_products(
        tile_work,
        measurement_jitter,
        measurement_readings,
        measurement_noise_spread,
        measurement_grid_location,
        active_tallies,
    )
    all_products = lax.all_gather(products, "obs", axis=0, tiled=True)
    obs_blocks = all_products.shape[0]
    block_links = coupling_listing[0]
    factor = taper_factors[0] / (members - 1)
    choose = block_links[..., None] == jnp.arange(obs_blocks, dtype=jnp.int32)
    localize = jnp.sum(jnp.where(choose, factor[..., None], jnp.float32(0.0)), axis=1)
    ensemble = jnp.einsum("bc,cmn->bmn", localize, all_products, precision=highest)
    region_dev = deviation.reshape(members, blocks, -1)
    increment = jnp.einsum("bmn,nbp->mbp", ensemble, region_dev, precision=highest)
    increment_low = increment.reshape(members, -1).astype(jnp.bfloat16)
    back = lax.all_to_all(increment_low, "slab", split_axis=0, concat_axis=1, tiled=True)
    return background_members + back.astype(jnp.float32)


def solution(mesh):
    return jax.shard_map(
        local,
        mesh=mesh,
        in_specs=(
            P("slab", "obs"),
            P(None, "obs", "slab"),
            P("obs", "slab"),
            P("obs", "slab"),
            P("obs", "slab"),
            P("obs", "slab"),
            P("obs", "slab", None),
            P("obs", "slab", None),
        ),
        out_specs=P("slab", "obs"),
        check_vma=False,
    )
```

profile of v0, /device:TPU:1, one launch (start us, length us, event | category | flops | bytes accessed | tf_op | source)
XLA Modules:
  0.0 124.3 jit_solution(9766494422847316278)
XLA Ops:
  6.5 0.0 copy-start.1
  6.5 0.0 copy-start.2
  6.5 1.4 %convert_element_type.60 = bf16[1,131072]{1,0:T(2,128)(2,1)S(1)} convert(f32[1,131072]{1,0:T(1,128)} %param.8) | non-fusion elementwise | flops 131072 | bytes 786432 | tf_op jit(solution)/shard_map/convert_element_type | solution.py:48
  8.0 0.5 broadcast.91
  8.5 2.1 %reduce.1 = bf16[64,2048]{1,0:T(8,128)(2,1)S(1)} reduce(bf16[64,1,2048]{2,1,0:T(2,128)(2,1)S(1)} %bitcast.46, bf16[]{:T(256)} %broadcast.91), dimensions={1}, to_apply=%bitcast.40.reduce_sub_computation | reduce | bytes 524290
  10.6 0.9 reshape.167
  11.5 14.8 %all-to-all-start = ((bf16[64,2,1024]{2,1,0:T(2,128)(2,1)}), bf16[64,2,1024]{2,1,0:T(2,128)(2,1)S(1)}, u32[]{:S(2)}, u32[]{:S(2)}) async-start(bf16[64,2,1024]{2,1,0:T(2,128)(2,1)} %reshape.167), calls=%async_computation | async-start | bytes 524288 | tf_op jit(solution)/shard_map/all_to_all | solution.py:49
  26.3 0.0 all-gather.2.cloned.1.call-start
  27.0 0.0 copy-done.1
  27.1 0.0 copy-done.2
  27.2 12.2 %all-to-all-done = bf16[64,2,1024]{2,1,0:T(2,128)(2,1)S(1)} async-done(((bf16[64,2,1024]{2,1,0:T(2,128)(2,1)}), bf16[64,2,1024]{2,1,0:T(2,128)(2,1)S(1)}, u32[]{:S(2)}, u32[]{:S(2)}) %all-to-all-start) | async-done | bytes 262176 | tf_op jit(solution)/shard_map/all_to_all | solution.py:49
  39.4 0.2 reshape.168
  39.7 0.5 copy.28
  40.2 0.1 convert_bitcast_fusion
  40.3 0.0 copy-start.3
  40.3 0.0 copy-start.6
  40.3 2.8 %gather_fusion = f32[1024,64]{1,0:T(8,128)S(1)} fusion(f32[64,2048]{0,1:T(8,128)S(1)} %convert_bitcast_fusion, s32[1024]{0:T(1024)S(1)} %broadcast_clamp_fusion), kind=kCustom, calls=%fused_computation | custom fusion | bytes 528384 | tf_op jit(solution)/shard_map/jit(_take)/gather | solution.py:21
  43.1 0.0 copy-start.5
  43.1 0.0 copy-start.4
  43.1 0.4 fusion.5
  43.5 0.5 multiply_reduce_fusion
  44.0 0.2 copy.32
  44.2 0.0 copy-done.3
  44.2 0.0 copy-done.6
  44.2 0.9 fusion.10
  45.2 0.0 all-gather.2.cloned.1.call-update
  45.2 0.0 copy-done.5
  45.2 0.1 copy.30
  45.3 0.0 copy-done.4
  45.3 0.1 copy.29
  45.4 0.1 select_reduce_fusion
  45.5 0.2 convert_reduce_fusion
  45.7 0.1 div.45
  45.8 34.1 %all-gather.2.cloned.1.call-done = f32[64,64,64]{2,1,0:T(8,128)} async-done(((f32[8,64,64]{2,1,0:T(8,128)}), f32[64,64,64]{2,1,0:T(8,128)}) %all-gather.2.cloned.1.call-update) | async-done | bytes 1048592 | tf_op jit(solution)/shard_map/all_gather | solution.py:62
  80.0 3.9 %fusion = f32[32,64,64]{2,0,1:T(8,128)S(1)} fusion(f32[64,64,64]{2,1,0:T(8,128)} %all-gather.2.cloned.1.call-done, f32[32,64]{1,0:T(8,128)S(1)} %select_reduce_fusion), kind=kOutput, calls=%fused_computation.1 | convolution fusion | flops 100663296 | bytes 1581056 | tf_op jit(solution)/shard_map/bc,cmn->bmn/dot_general | solution.py:68
  83.8 2.3 %convolution_convert_fusion = bf16[32,64,64]{2,1,0:T(8,128)(2,1)S(1)} fusion(f32[32,64,64]{2,0,1:T(8,128)S(1)} %fusion, f32[32,64]{1,0:T(8,128)S(1)} %div.45, bf16[64,32,64]{0,2,1:T(8,128)(2,1)S(1)} %bitcast.43), kind=kOutput, calls=%fused_computation.3 | convolution fusion | flops 101056512 | bytes 1056768 | tf_op jit(solution)/shard_map/bmn,nbp->mbp/dot_general | solution.py:70
  86.2 0.0 copy-start
  86.2 1.1 reduce.2
  87.3 0.2 copy.51
  87.5 0.2 reshape.169
  87.7 28.1 %all_to_all.23 = bf16[64,2,1024]{2,1,0:T(2,128)(2,1)S(1)} all-to-all(bf16[64,2,1024]{2,1,0:T(2,128)(2,1)S(1)} %reshape.169), channel_id=1, replica_groups=mesh['slab'=64,'obs'=8] {'slab'}, dimensions={0} | all-to-all | bytes 524288 | tf_op jit(solution)/shard_map/all_to_all | solution.py:72
  115.8 0.2 reshape.170
  116.0 0.0 copy-done
  116.0 1.5 %convert_add_fusion = f32[1,131072]{1,0:T(1,128)} fusion(f32[1,131072]{1,0:T(1,128)S(1)} %copy-done, bf16[1,131072]{1,0:T(2,128)(2,1)S(1)} %bitcast.45), kind=kLoop, calls=%fused_computation.6 | loop fusion | flops 262144 | bytes 1310720 | tf_op jit(solution)/shard_map/add | solution.py:73
  (11 shorter events, 0.1 us)
Async XLA Ops:
  6.5 20.5 %copy-start.1 = (bf16[64,1,1024]{2,0,1:T(8,128)(2,1)S(1)}, bf16[64,1,1024]{2,0,1:T(8,128)(2,1)}, u32[]{:S(2)}) copy-start(bf16[64,1,1024]{2,0,1:T(8,128)(2,1)} %param.9) | copy-start | bytes 393220
  6.5 20.5 %copy-start.2 = (s32[1,1024]{1,0:T(1,128)S(1)}, s32[1,1024]{1,0:T(1,128)}, u32[]{:S(2)}) copy-start(s32[1,1024]{1,0:T(1,128)} %param.12) | copy-start | bytes 12292
  11.5 27.9 %all-to-all-start = ((bf16[64,2,1024]{2,1,0:T(2,128)(2,1)}), bf16[64,2,1024]{2,1,0:T(2,128)(2,1)S(1)}, u32[]{:S(2)}, u32[]{:S(2)}) async-start(bf16[64,2,1024]{2,1,0:T(2,128)(2,1)} %reshape.167), calls=%async_computation | async-start | bytes 524288 | tf_op jit(solution)/shard_map/all_to_all | solution.py:49
  26.3 53.6 %all-gather.2.cloned.1.call-start = ((), (), s32[]{:S(2)}) async-start(), calls=%async_computation.2 | async-start | bytes 2359296 | tf_op jit(solution)/shard_map/all_gather | solution.py:62
  40.3 4.0 %copy-start.3 = (f32[1,1024]{1,0:T(1,128)S(1)}, f32[1,1024]{1,0:T(1,128)}, u32[]{:S(2)}) copy-start(f32[1,1024]{1,0:T(1,128)} %param.11) | copy-start | bytes 12292
  40.3 4.0 %copy-start.6 = (f32[1,1024]{1,0:T(1,128)S(1)}, f32[1,1024]{1,0:T(1,128)}, u32[]{:S(2)}) copy-start(f32[1,1024]{1,0:T(1,128)} %param.10) | copy-start | bytes 12292
  43.1 2.1 %copy-start.5 = (f32[1,32,8]{1,2,0:T(8,128)S(1)}, f32[1,32,8]{1,2,0:T(8,128)}, u32[]{:S(2)}) copy-start(f32[1,32,8]{1,2,0:T(8,128)} %param.15) | copy-start | bytes 3076
  43.1 2.2 %copy-start.4 = (s32[1,32,8]{1,2,0:T(8,128)S(1)}, s32[1,32,8]{1,2,0:T(8,128)}, u32[]{:S(2)}) copy-start(s32[1,32,8]{1,2,0:T(8,128)} %param.14) | copy-start | bytes 3076
  86.2 29.8 %copy-start = (f32[1,131072]{1,0:T(1,128)S(1)}, f32[1,131072]{1,0:T(1,128)}, u32[]{:S(2)}) copy-start(f32[1,131072]{1,0:T(1,128)} %param.8) | copy-start | bytes 1572868
Sparse Core Ops, SparseCore 0:
  45.3 34.6 all-gather.1
where the time goes:
time: 125 us; the launch traced here: 124 us
  waiting for transfers between devices  46.4 us (37%)
  blocking collectives  28.1 us (22%)
  starting transfers between devices  14.9 us (12%)
  between operations  14.3 us (11%)
  other arithmetic  7.54 us (6%)
  matrix products  7.11 us (6%)
  local copies, waits for them, and re-layouts  6.04 us (5%)
    all_gather x1, waiting for transfers between devices, local(): all_products = lax.all_gather(products, 'obs', axis=0, tiled=True)  34.1 us
    all_to_all x1, blocking collectives, local(): lax.all_to_all(increment_low, 'slab', split_axis=0, concat_axis=1, tiled=...  28.1 us
    all_to_all x1, starting transfers between devices, local(): lax.all_to_all(work_low, 'slab', split_axis=1, concat_axis=0, tiled=True)  14.8 us
    all_to_all x1, waiting for transfers between devices, local(): lax.all_to_all(work_low, 'slab', split_axis=1, concat_axis=0, tiled=True)  12.2 us
    dot_general x1, matrix products, local(): jnp.einsum('bc,cmn->bmn', localize, all_products, precision=highest)  3.85 us
    gather x2, local copies, waits for them, and re-layouts, block_products(): prior_value = jnp.take(tile_work, positions, axis=1)  2.99 us
  transfers between devices with their start and end apart: 2, of which 2 were waited for; matrix products, arithmetic and copies ran while one was open for 1% of the time, Pallas kernels for 0%

commit v1 on v0

--- a/solution.py
+++ b/solution.py
@@ -59,7 +59,9 @@
         measurement_grid_location,
         active_tallies,
     )
-    all_products = lax.all_gather(products, "obs", axis=0, tiled=True)
+    all_products = jnp.concatenate(
+        lax.all_to_all(jnp.stack([products] * lax.axis_size("obs")), "obs", 0, 0), axis=0
+    )
     obs_blocks = all_products.shape[0]
     block_links = coupling_listing[0]
     factor = taper_factors[0] / (members - 1)

time: 125 us -> 108 us (0.86)
  between operations: 14.3 us -> 0.95 us
  blocking collectives: 28.1 us -> 17.6 us
  starting transfers between devices: 14.9 us -> 21.6 us
  waiting for transfers between devices: 46.4 us -> 40.9 us
  local copies, waits for them, and re-layouts: 6.04 us -> 11.1 us
  other arithmetic: 7.54 us -> 12.2 us
  matrix products: 7.11 us -> 3.67 us
    all_gather x1 -> x0, waiting for transfers between devices: 34.1 us -> none  [local(): all_products = lax.all_gather(products, 'obs', axis=0, tiled=True)]
    all_to_all x0 -> x1, waiting for transfers between devices: none -> 28.6 us  [local(): lax.all_to_all(jnp.stack([products] * lax.axis_size('obs')), 'obs', 0, 0)]
    all_to_all x1, blocking collectives: 28.1 us -> 17.6 us  [local(): lax.all_to_all(increment_low, 'slab', split_axis=0, concat_axis=1, tiled=...]
    all_to_all x0 -> x1, starting transfers between devices: none -> 6.82 us  [local(): lax.all_to_all(jnp.stack([products] * lax.axis_size('obs')), 'obs', 0, 0)]
    all_to_all x0 -> x1, other arithmetic: none -> 4.52 us  [local(): lax.all_to_all(jnp.stack([products] * lax.axis_size('obs')), 'obs', 0, 0)]
    unnamed x21 -> x24, local copies, waits for them, and re-layouts: 2.31 us -> 6.72 us
    dot_general x1, matrix products: 3.85 us -> 1.11 us  [local(): jnp.einsum('bc,cmn->bmn', localize, all_products, precision=highest)]
where the time goes in v1:
time: 108 us
  waiting for transfers between devices  40.9 us (38%)
  starting transfers between devices  21.6 us (20%)
  blocking collectives  17.6 us (16%)
  other arithmetic  12.2 us (11%)
  local copies, waits for them, and re-layouts  11.1 us (10%)
  matrix products  3.67 us (3%)
    all_to_all x1, waiting for transfers between devices, local(): lax.all_to_all(jnp.stack([products] * lax.axis_size('obs')), 'obs', 0, 0)  28.6 us
    all_to_all x1, blocking collectives, local(): lax.all_to_all(increment_low, 'slab', split_axis=0, concat_axis=1, tiled=...  17.6 us
    all_to_all x1, starting transfers between devices, local(): lax.all_to_all(work_low, 'slab', split_axis=1, concat_axis=0, tiled=True)  14.8 us
    all_to_all x1, waiting for transfers between devices, local(): lax.all_to_all(work_low, 'slab', split_axis=1, concat_axis=0, tiled=True)  12.3 us
    all_to_all x1, starting transfers between devices, local(): lax.all_to_all(jnp.stack([products] * lax.axis_size('obs')), 'obs', 0, 0)  6.82 us
    unnamed x24, local copies, waits for them, and re-layouts  6.72 us
    all_to_all x1, other arithmetic, local(): lax.all_to_all(jnp.stack([products] * lax.axis_size('obs')), 'obs', 0, 0)  4.52 us
    gather x2, local copies, waits for them, and re-layouts, block_products(): prior_value = jnp.take(tile_work, positions, axis=1)  2.99 us
  transfers between devices with their start and end apart: 2, of which 2 were waited for; matrix products, arithmetic and copies ran while one was open for 1% of the time, Pallas kernels for 0%

profile of v1, /device:TPU:1, one launch (start us, length us, event | category | flops | bytes accessed | tf_op | source)
XLA Modules:
  0.0 108.1 jit_solution(8541478088746418677)
XLA Ops:
  0.0 0.0 copy-start.1
  0.0 1.4 %convert_element_type.60 = bf16[1,131072]{1,0:T(2,128)(2,1)S(1)} convert(f32[1,131072]{1,0:T(1,128)} %param.8) | non-fusion elementwise | flops 131072 | bytes 786432 | tf_op jit(solution)/shard_map/convert_element_type | solution.py:48
  1.4 0.6 broadcast.93
  2.0 2.2 %reduce.1 = bf16[64,2048]{1,0:T(8,128)(2,1)S(1)} reduce(bf16[64,1,2048]{2,1,0:T(2,128)(2,1)S(1)} %bitcast.55, bf16[]{:T(256)} %broadcast.93), dimensions={1}, to_apply=%bitcast.43.reduce_sub_computation | reduce | bytes 524290
  4.2 0.9 reshape.173
  5.1 14.8 %all-to-all-start = ((bf16[64,2,1024]{2,1,0:T(2,128)(2,1)}), bf16[64,2,1024]{2,1,0:T(2,128)(2,1)S(1)}, u32[]{:S(2)}, u32[]{:S(2)}) async-start(bf16[64,2,1024]{2,1,0:T(2,128)(2,1)} %reshape.173), calls=%async_computation | async-start | bytes 524288 | tf_op jit(solution)/shard_map/all_to_all | solution.py:49
  20.6 0.0 copy-done.1
  20.6 0.0 copy-done.2
  20.8 12.3 %all-to-all-done = bf16[64,2,1024]{2,1,0:T(2,128)(2,1)S(1)} async-done(((bf16[64,2,1024]{2,1,0:T(2,128)(2,1)}), bf16[64,2,1024]{2,1,0:T(2,128)(2,1)S(1)}, u32[]{:S(2)}, u32[]{:S(2)}) %all-to-all-start) | async-done | bytes 262176 | tf_op jit(solution)/shard_map/all_to_all | solution.py:49
  33.0 0.2 reshape.174
  33.3 0.5 copy.40
  33.8 0.1 convert_bitcast_fusion
  33.9 0.0 copy-start.3
  33.9 0.0 copy-start.6
  33.9 2.8 %gather_fusion = f32[1024,64]{1,0:T(8,128)S(1)} fusion(f32[64,2048]{0,1:T(8,128)S(1)} %convert_bitcast_fusion, s32[1024]{0:T(1024)S(1)} %broadcast_clamp_fusion), kind=kCustom, calls=%fused_computation | custom fusion | bytes 528384 | tf_op jit(solution)/shard_map/jit(_take)/gather | solution.py:21
  36.7 0.4 fusion.6
  37.1 0.5 multiply_reduce_fusion
  37.6 0.2 copy.44
  37.8 0.0 copy-done.3
  37.8 0.0 copy-done.6
  37.8 0.2 fusion.11
  38.0 0.2 copy.45
  38.2 0.1 broadcast_bitcast_fusion
  38.4 0.0 copy-start.5
  38.4 0.0 copy-start.4
  38.4 2.1 %reshape.175 = f32[8,1,32768]{2,1,0:T(1,128)} reshape(f32[8,64,8,64]{3,2,1,0:T(8,128)S(1)} %broadcast_bitcast_fusion) | data formatting | bytes 2097152
  40.5 6.8 %all-to-all-start.1 = ((f32[8,1,32768]{2,1,0:T(1,128)}), f32[8,1,32768]{2,1,0:T(1,128)S(1)}, u32[]{:S(2)}, u32[]{:S(2)}) async-start(f32[8,1,32768]{2,1,0:T(1,128)} %reshape.175), calls=%async_computation.1 | async-start | bytes 2097152 | tf_op jit(solution)/shard_map/all_to_all | solution.py:63
  47.3 0.0 copy-done.5
  47.4 0.1 copy.42
  47.4 0.0 copy-done.4
  47.4 0.1 copy.41
  47.5 0.1 select_reduce_fusion
  47.7 0.2 convert_reduce_fusion
  47.9 0.1 div.45
  48.0 28.6 %all-to-all-done.1 = f32[8,1,32768]{2,1,0:T(1,128)S(1)} async-done(((f32[8,1,32768]{2,1,0:T(1,128)}), f32[8,1,32768]{2,1,0:T(1,128)S(1)}, u32[]{:S(2)}, u32[]{:S(2)}) %all-to-all-start.1) | async-done | bytes 1048608 | tf_op jit(solution)/shard_map/all_to_all | solution.py:63
  76.6 0.5 broadcast.94
  77.1 4.5 %reduce.2 = f32[8,32768]{1,0:T(8,128)} reduce(f32[8,1,32768]{2,1,0:T(1,128)S(1)} %all-to-all-done.1, f32[]{:T(128)} %broadcast.94), dimensions={1}, to_apply=%all_to_all.23.reduce_sub_computation | reduce | bytes 2097156 | tf_op jit(solution)/shard_map/all_to_all | solution.py:63
  81.6 2.1 %reshape.176 = f32[8,64,8,64]{3,2,1,0:T(8,128)S(1)} reshape(f32[8,32768]{1,0:T(8,128)} %reduce.2) | data formatting | bytes 2097152
  83.7 1.1 %fusion = f32[32,64,64]{2,0,1:T(8,128)S(1)} fusion(f32[32,64]{1,0:T(8,128)S(1)} %select_reduce_fusion, f32[8,64,8,64]{3,2,1,0:T(8,128)S(1)} %reshape.176), kind=kOutput, calls=%fused_computation.1 | convolution fusion | flops 100663296 | bytes 1581056 | tf_op jit(solution)/shard_map/bc,cmn->bmn/dot_general | solution.py:70
  84.8 2.3 %convolution_convert_fusion = bf16[32,64,64]{2,1,0:T(8,128)(2,1)S(1)} fusion(f32[32,64,64]{2,0,1:T(8,128)S(1)} %fusion, f32[32,64]{1,0:T(8,128)S(1)} %div.45, bf16[64,32,64]{0,2,1:T(8,128)(2,1)S(1)} %bitcast.52), kind=kOutput, calls=%fused_computation.4 | convolution fusion | flops 101056512 | bytes 1056768 | tf_op jit(solution)/shard_map/bmn,nbp->mbp/dot_general | solution.py:72
  87.2 0.0 copy-start
  87.2 1.2 %reduce.3 = bf16[64,2048]{0,1:T(8,128)(2,1)S(1)} reduce(bf16[64,1,2048]{0,2,1:T(8,128)(2,1)S(1)} %bitcast.57, bf16[]{:T(256)} %broadcast.93), dimensions={1}, to_apply=%copy.48.reduce_sub_computation | reduce | bytes 524290 | tf_op jit(solution)/shard_map/convert_element_type | solution.py:73
  88.4 0.2 copy.66
  88.6 0.2 reshape.177
  88.8 17.6 %all_to_all.28 = bf16[64,2,1024]{2,1,0:T(2,128)(2,1)S(1)} all-to-all(bf16[64,2,1024]{2,1,0:T(2,128)(2,1)S(1)} %reshape.177), channel_id=1, replica_groups=mesh['slab'=64,'obs'=8] {'slab'}, dimensions={0} | all-to-all | bytes 524288 | tf_op jit(solution)/shard_map/all_to_all | solution.py:74
  106.4 0.2 reshape.178
  106.6 0.0 copy-done
  106.6 1.5 %convert_add_fusion = f32[1,131072]{1,0:T(1,128)} fusion(f32[1,131072]{1,0:T(1,128)S(1)} %copy-done, bf16[1,131072]{1,0:T(2,128)(2,1)S(1)} %bitcast.54), kind=kLoop, calls=%fused_computation.7 | loop fusion | flops 262144 | bytes 1310720 | tf_op jit(solution)/shard_map/add | solution.py:75
  (12 shorter events, 0.1 us)
Async XLA Ops:
  0.0 20.6 %copy-start.1 = (bf16[64,1,1024]{2,0,1:T(8,128)(2,1)S(1)}, bf16[64,1,1024]{2,0,1:T(8,128)(2,1)}, u32[]{:S(2)}) copy-start(bf16[64,1,1024]{2,0,1:T(8,128)(2,1)} %param.9) | copy-start | bytes 393220
  0.0 20.6 %copy-start.2 = (s32[1,1024]{1,0:T(1,128)S(1)}, s32[1,1024]{1,0:T(1,128)}, u32[]{:S(2)}) copy-start(s32[1,1024]{1,0:T(1,128)} %param.12) | copy-start | bytes 12292
  5.1 27.9 %all-to-all-start = ((bf16[64,2,1024]{2,1,0:T(2,128)(2,1)}), bf16[64,2,1024]{2,1,0:T(2,128)(2,1)S(1)}, u32[]{:S(2)}, u32[]{:S(2)}) async-start(bf16[64,2,1024]{2,1,0:T(2,128)(2,1)} %reshape.173), calls=%async_computation | async-start | bytes 524288 | tf_op jit(solution)/shard_map/all_to_all | solution.py:49
  33.9 3.9 %copy-start.3 = (f32[1,1024]{1,0:T(1,128)S(1)}, f32[1,1024]{1,0:T(1,128)}, u32[]{:S(2)}) copy-start(f32[1,1024]{1,0:T(1,128)} %param.11) | copy-start | bytes 12292
  33.9 3.9 %copy-start.6 = (f32[1,1024]{1,0:T(1,128)S(1)}, f32[1,1024]{1,0:T(1,128)}, u32[]{:S(2)}) copy-start(f32[1,1024]{1,0:T(1,128)} %param.10) | copy-start | bytes 12292
  38.4 9.0 %copy-start.5 = (f32[1,32,8]{1,2,0:T(8,128)S(1)}, f32[1,32,8]{1,2,0:T(8,128)}, u32[]{:S(2)}) copy-start(f32[1,32,8]{1,2,0:T(8,128)} %param.15) | copy-start | bytes 3076
  38.4 9.1 %copy-start.4 = (s32[1,32,8]{1,2,0:T(8,128)S(1)}, s32[1,32,8]{1,2,0:T(8,128)}, u32[]{:S(2)}) copy-start(s32[1,32,8]{1,2,0:T(8,128)} %param.14) | copy-start | bytes 3076
  40.5 36.1 %all-to-all-start.1 = ((f32[8,1,32768]{2,1,0:T(1,128)}), f32[8,1,32768]{2,1,0:T(1,128)S(1)}, u32[]{:S(2)}, u32[]{:S(2)}) async-start(f32[8,1,32768]{2,1,0:T(1,128)} %reshape.175), calls=%async_computation.1 | async-start | bytes 2097152 | tf_op jit(solution)/shard_map/all_to_all | solution.py:63
  87.2 19.4 %copy-start = (f32[1,131072]{1,0:T(1,128)S(1)}, f32[1,131072]{1,0:T(1,128)}, u32[]{:S(2)}) copy-start(f32[1,131072]{1,0:T(1,128)} %param.8) | copy-start | bytes 1572868
